TPU v7x, 32 devices: a whole 2x2x4 slice. The times are simulated.
32 devices in a mesh: group: 2 (over y), seq: 8 (over z, x), head: 2 (over core).
Axes of the slice: x: 2, y: 2, z: 4, core: 2. Of those that a mesh axis runs over, the one named last changes fastest.
Arguments:
- x_in: bfloat16 [4096, 4096], P(('group', 'seq'), 'head'), parts along dimension 0, may hold values from -6 to 6
- step_size: float32 [64, 4096], P('head', ('group', 'seq')), parts along dimension 1, may hold values from 0.002 to 0.128
- a_log: float32 [64], P('head'), may hold values from -8.5 to 0.9
- d_skip: float32 [64], P('head'), may hold values from 0.1 to 1.9
- b_in: bfloat16 [4096, 128], P(('group', 'seq')), parts along dimension 0, may hold values from -6 to 6
- c_in: bfloat16 [4096, 128], P(('group', 'seq')), parts along dimension 0, may hold values from -0.52734375 to 0.52734375
- queries: bfloat16 [4096, 2048], P(('group', 'seq'), 'head'), parts along dimension 0, may hold values from -4.5 to 4.5
- key_rows: bfloat16 [4096, 512], P(('group', 'seq'), 'head'), parts along dimension 0, may hold values from -4.5 to 4.5
- values: bfloat16 [4096, 512], P(('group', 'seq'), 'head'), parts along dimension 0, may hold values from -6 to 6
Outputs:
- mamba_out: bfloat16 [4096, 4096], P(('group', 'seq'), 'head'), parts along dimension 0
- attn_out: bfloat16 [4096, 2048], P(('group', 'seq'), 'head'), parts along dimension 0
There are 2 independent parts, one for each index of `group`. A program takes and returns all parts, laid end to end along the dimension named above; an argument that names none is the same for every part. Nothing has to cross between parts.
All inputs are finite; a program needn't handle non-finite values.
Results may differ from a plain program's by a relative error of at most 0.009.
Values may be sent and summed in bfloat16 or wider, within the bound.
No kernel may reach another device: no remote copies, remote signals or barrier semaphores. Data moves between devices by JAX's collectives and lax.ppermute only.
A program may use at most 320 MiB of HBM per device.

v0:
```python
import jax
import jax.numpy as jnp
from jax import lax
from jax.sharding import PartitionSpec as P

BLOCK = 128
HEADDIM = 64
STATE = 128
QHEADS = 16
KVHEADS = 4
HD = 128
NEG = -1e30


def carried_in(value, axis, combine, identity):
    count, mine = (lax.axis_size(axis), lax.axis_index(axis))
    everything = jax.tree.map(
        lambda part, kind: lax.all_gather(part.astype(kind), axis),
        value,
        (jnp.bfloat16, jnp.bfloat16),
    )
    start = jax.tree.map(
        lambda part, zero: jnp.broadcast_to(jnp.asarray(zero, part.dtype), part.shape),
        value,
        identity,
    )

    def turn(k, before):
        reached = k < mine
        new = combine(
            before, jax.tree.map(lambda part, own: part[k].astype(own.dtype), everything, value)
        )
        return jax.tree.map(lambda a, b: jnp.where(reached, a, b), new, before)

    return lax.fori_loop(0, count, turn, start)


def broadcast(value, axis, source):
    kept = jnp.where(lax.axis_index(axis) == source, value, 0).astype(value.dtype)
    return lax.psum(kept, axis)


def ssd_local(x_blocks, steps, rate, b_blocks, c_blocks):
    cum = jnp.cumsum(steps * rate[None, :, None], axis=2)
    causal = jnp.arange(BLOCK)[:, None] >= jnp.arange(BLOCK)[None, :]
    log_gap = jnp.where(causal, cum[:, :, :, None] - cum[:, :, None, :], -jnp.inf)
    inner = jnp.einsum("cin,cjn->cij", c_blocks, b_blocks, preferred_element_type=jnp.float32)
    mixing = (inner[:, None] * jnp.exp(log_gap) * steps[:, :, None, :]).astype(jnp.bfloat16)
    intra = jnp.einsum("chij,cjhp->cihp", mixing, x_blocks, preferred_element_type=jnp.float32)
    log_total = cum[:, :, -1]
    factor = (jnp.exp(log_total[:, :, None] - cum) * steps).transpose(0, 2, 1)[..., None]
    scaled = (factor * x_blocks.astype(jnp.float32)).astype(jnp.bfloat16)
    block_state = jnp.einsum("cjhp,cjn->chpn", scaled, b_blocks, preferred_element_type=jnp.float32)
    return (intra, block_state, log_total, cum)


def ssd_finish(intra, cum, c_blocks, incoming, d_skip, x_blocks):
    carried = jnp.einsum(
        "cin,chpn->cihp", c_blocks.astype(jnp.float32), incoming, precision=lax.Precision.HIGHEST
    )
    carried = carried * jnp.exp(cum).transpose(0, 2, 1)[..., None]
    return (intra + carried + d_skip[None, None, :, None] * x_blocks.astype(jnp.float32)).astype(
        jnp.bfloat16
    )


def chain(earlier, later):
    return (earlier[0] * later[0], later[0][..., None, None] * earlier[1] + later[1])


def local(x_in, step_size, a_log, d_skip, b_in, c_in, queries, key_rows, values):
    my_index = lax.axis_index("seq")
    seq_count = lax.axis_size("seq")
    tok_rows = x_in.shape[0]
    slots = tok_rows // BLOCK
    mamba_local = step_size.shape[0]
    rate = -jnp.exp(a_log)
    x_blocks = x_in.reshape(slots, BLOCK, mamba_local, HEADDIM)
    steps = step_size.reshape(mamba_local, slots, BLOCK).transpose(1, 0, 2)
    b_blocks = b_in.reshape(slots, BLOCK, STATE)
    c_blocks = c_in.reshape(slots, BLOCK, STATE)
    intra, block_state, log_total, cum = ssd_local(x_blocks, steps, rate, b_blocks, c_blocks)
    decay = jnp.exp(log_total)
    identity = (jnp.ones_like(decay), jnp.zeros_like(block_state))
    prefix = carried_in((decay, block_state), "seq", chain, identity)
    inclusive = chain(prefix, (decay, block_state))
    total_decay, total_state = (
        broadcast(inclusive[0].astype(jnp.bfloat16), "seq", lax.axis_size("seq") - 1).astype(
            jnp.float32
        ),
        broadcast(inclusive[1].astype(jnp.bfloat16), "seq", lax.axis_size("seq") - 1).astype(
            jnp.float32
        ),
    )
    carry_state = jnp.zeros_like(block_state[0])
    entering = []
    for slot in range(slots):
        entering.append(prefix[0][slot][:, None, None] * carry_state + prefix[1][slot])
        carry_state = total_decay[slot][:, None, None] * carry_state + total_state[slot]
    incoming = jnp.stack(entering, axis=0)
    mamba_out = ssd_finish(intra, cum, c_blocks, incoming, d_skip, x_blocks).reshape(
        tok_rows, mamba_local * HEADDIM
    )
    per_kv = QHEADS // KVHEADS
    kv_local = key_rows.shape[1] // HD
    score_scale = 1.0 / HD**0.5
    stride = seq_count * BLOCK
    q_flat = queries.reshape(slots, BLOCK, kv_local, per_kv, HD).transpose(2, 0, 3, 1, 4)
    q_flat = q_flat.reshape(kv_local, slots * per_kv * BLOCK, HD)
    q_slot = jnp.arange(slots)[:, None, None]
    q_row = jnp.arange(BLOCK)[None, None, :]
    query_pos = (
        q_slot * stride + my_index * BLOCK + q_row + jnp.zeros((slots, per_kv, BLOCK), jnp.int32)
    ).reshape(-1)
    k_slots = key_rows.reshape(slots, BLOCK, kv_local * HD)
    v_slots = values.reshape(slots, BLOCK, kv_local * HD)
    q_total = slots * per_kv * BLOCK
    start_state = (
        jnp.full((kv_local, q_total), NEG, jnp.float32),
        jnp.zeros((kv_local, q_total), jnp.float32),
        jnp.zeros((kv_local, q_total, HD), jnp.float32),
    )
    running = start_state
    k_piece = lax.all_gather(k_slots, "seq", axis=1, tiled=True)
    v_piece = lax.all_gather(v_slots, "seq", axis=1, tiled=True)
    rows = k_piece.shape[1]
    block_rows = 512
    count = rows // block_rows
    k_blocks = k_piece.reshape(slots, count, block_rows, kv_local, HD).transpose(1, 0, 2, 3, 4)
    v_blocks = v_piece.reshape(slots, count, block_rows, kv_local, HD).transpose(1, 0, 2, 3, 4)
    k_slot = jnp.arange(slots)[:, None]
    k_row = jnp.arange(block_rows)[None, :]

    def per_block(state, inputs):
        k_block, v_block, number = inputs
        run_max, run_sum, run_acc = state
        k_flat = k_block.reshape(slots * block_rows, kv_local, HD)
        v_flat = v_block.reshape(slots * block_rows, kv_local, HD)
        key_pos = (k_slot * stride + number * block_rows + k_row).reshape(-1)
        visible = key_pos[None, None, :] <= query_pos[None, :, None]
        scores = (
            jnp.einsum("gqd,kgd->gqk", q_flat, k_flat, preferred_element_type=jnp.float32)
            * score_scale
        )
        scores = jnp.where(visible, scores, NEG)
        new_max = jnp.maximum(run_max, jnp.max(scores, axis=-1))
        rescale = jnp.exp(run_max - new_max)
        weights = jnp.where(visible, jnp.exp(scores - new_max[..., None]), 0.0)
        new_sum = run_sum * rescale + jnp.sum(weights, axis=-1)
        update = jnp.einsum(
            "gqk,kgd->gqd", weights.astype(jnp.bfloat16), v_flat, preferred_element_type=jnp.float32
        )
        return ((new_max, new_sum, run_acc * rescale[..., None] + update), None)

    numbers = jnp.arange(count)
    running, unused = lax.scan(per_block, running, (k_blocks, v_blocks, numbers))
    run_max, run_sum, run_acc = running
    attended = (run_acc / run_sum[..., None]).astype(jnp.bfloat16)
    attn_out = (
        attended.reshape(kv_local, slots, per_kv, BLOCK, HD)
        .transpose(1, 3, 0, 2, 4)
        .reshape(tok_rows, kv_local * per_kv * HD)
    )
    return (mamba_out, attn_out)


def solution(mesh):
    in_specs = (
        P(("group", "seq"), "head"),
        P("head", ("group", "seq")),
        P("head"),
        P("head"),
        P(("group", "seq"), None),
        P(("group", "seq"), None),
        P(("group", "seq"), "head"),
        P(("group", "seq"), "head"),
        P(("group", "seq"), "head"),
    )
    out_specs = (P(("group", "seq"), "head"), P(("group", "seq"), "head"))
    return jax.shard_map(local, mesh=mesh, in_specs=in_specs, out_specs=out_specs, check_vma=False)
```

profile of v0, /device:TPU:0, one launch (start us, length us, event | category | flops | bytes accessed | tf_op | source)
XLA Modules:
  0.0 329.5 jit_solution(400362677163292108)
XLA Ops:
  7.2 0.7 all-gather.6.cloned.1.call-update
  8.0 0.7 all-gather.8.cloned.1.call-update
  8.7 0.7 exponential_negate_fusion
  9.4 0.8 broadcast_multiply_fusion
  10.2 0.6 reduce_window_sum.11
  10.8 0.1 slice.36
  10.9 0.1 copy.65
  10.9 3.3 %reshape.215 = bf16[2,128,32,64]{3,2,1,0:T(8,128)(2,1)S(1)} reshape(bf16[256,2048]{1,0:T(8,128)(2,1)} %param.13) | data formatting | bytes 2097152 | tf_op jit(solution)/shard_map/reshape | solution.py:78
  14.3 2.2 copy.44
  16.5 0.1 fusion.45
  16.6 2.1 fusion.48
  18.9 22.4 %all-gather = bf16[16,32,1]{1,2,0:T(2,128)(2,1)S(1)} all-gather(bf16[2,32,1]{1,2,0:T(2,128)(2,1)S(1)} %copy.46), channel_id=2, replica_groups=mesh['group'=2,'seq'=8,'head'=2] {'seq'}, dimensions={0}, use_global_device_ids=true | all-gather | bytes 1152 | tf_op jit(solution)/shard_map/all_gather | solution.py:18
  41.4 2.2 reshape.198
  43.6 2.0 copy.50
  45.5 0.1 iota_add_fusion.1
  45.7 0.2 fusion.49
  45.8 3.4 %fusion.24 = f32[2,32,128,64]{2,3,1,0:T(8,128)} fusion(bf16[2,128,32,64]{1,3,2,0:T(8,128)(2,1)S(1)} %copy.44, f32[2,32,128]{2,1,0:T(8,128)S(1)} %bitcast_bitcast_fusion.1, f32[2,32,128]{2,1,0:T(8,128)S(1)} %reduce_window_sum.11, f32[2,128,128]{2,1,0:T(8,128)S(1)} %fusion.49, pred[128,128]{1,0:T(8,128)(4,1)S(1)} %iota_compare_fusion), kind=kOutput, calls=%fused_computation.35 | convolution fusion | flops 139460608 | bytes 3358720 | tf_op jit(solution)/shard_map/chij,cjhp->cihp/dot_general | solution.py:49
  49.2 4.0 %all-gather.6.cloned.1.call-done = bf16[2,1024,256]{2,1,0:T(8,128)(2,1)} async-done(((bf16[2,128,256]{2,1,0:T(8,128)(2,1)}), bf16[2,1024,256]{2,1,0:T(8,128)(2,1)}) %all-gather.6.cloned.1.call-update) | async-done | bytes 1048592 | tf_op jit(solution)/shard_map/all_gather | solution.py:124
  53.1 2.2 reshape.197
  55.4 39.0 %all-gather.8.cloned.1.call-done = bf16[2,1024,256]{2,1,0:T(8,128)(2,1)} async-done(((bf16[2,128,256]{2,1,0:T(8,128)(2,1)}), bf16[2,1024,256]{2,1,0:T(8,128)(2,1)}) %all-gather.8.cloned.1.call-update) | async-done | bytes 1048592 | tf_op jit(solution)/shard_map/all_gather | solution.py:125
  94.3 2.1 reshape.201
  96.4 123.7 %all-gather.10.cloned.1.call-done = bf16[16,32,64,128]{3,2,1,0:T(8,128)(2,1)} async-done(((bf16[2,32,64,128]{3,2,1,0:T(8,128)(2,1)}), bf16[16,32,64,128]{3,2,1,0:T(8,128)(2,1)}) %all-gather.10.cloned.1.call-update) | async-done | bytes 8388624 | tf_op jit(solution)/shard_map/all_gather | solution.py:18
  220.2 14.6 %while.31 = (s32[]{:T(128)}, f32[2,32]{1,0:T(2,128)S(1)}, f32[2,32,64,128]{3,2,1,0:T(8,128)S(1)}, s32[]{:T(128)}, bf16[8,2,32]{2,1,0:T(2,128)(2,1)S(1)}, /*index...) while((s32[]{:T(128)}, f32[2,32]{1,0:T(2,128)S(1)}, f32[2,32,64,128]{3,2,1,0:T(8,128)S(1)}, ...), condition=%wide.region_2.3_spmd.clone, body=%wide.region_1.2_spmd.clone.sunk | while | flops 2621764 | bytes 5244279 | solution.py:35
  220.2 1.8 fusion.73
  222.0 1.8 fusion.73
  223.8 1.8 fusion.73
  225.6 1.8 fusion.73
  227.5 1.8 fusion.73
  229.3 1.8 fusion.73
  231.1 1.8 fusion.73
  232.9 1.8 fusion.73
  234.8 3.0 fusion.41
  237.7 41.9 %while.32 = (s32[]{:T(128)}, f32[2,1024]{1,0:T(2,128)S(1)}, f32[2,1024]{1,0:T(2,128)S(1)}, f32[2,1024,128]{2,1,0:T(8,128)}, s32[2]{0:T(128)S(1)}, /*index=5*/bf1...) while((s32[]{:T(128)}, f32[2,1024]{1,0:T(2,128)S(1)}, ...), condition=%wide.region_8.9_spmd.clone, body=%wide.region_5.8_spmd.clone.sunk | while | flops 1102851072 | bytes 83518768 | solution.py:156
  237.8 0.6 dynamic_slice.45
  239.0 0.1 fusion.79
  239.1 0.7 broadcast_compare_fusion.2
  239.7 2.7 constant_dynamic-slice_fusion.3
  242.6 5.0 %fusion.80 = (f32[2,1024]{1,0:T(2,128)S(1)}, f32[2,1024,1024]{2,1,0:T(8,128)}) fusion(pred[1024,1024]{0,1:T(8,128)(4,1)S(1)} %broadcast_compare_fusion.2, bf16[1024,2,128]{2,0,1:T(8,128)(2,1)S(1)} %bitcast.142, bf16[2,1024,128]{2,1,0:T(8,128)(2,1)S(1)} %copy-done.8), kind=kOutput, calls=%fused_computation.9.clone.1 | convolution fusion | flops 543160320 | bytes 10493952 | tf_op jit(solution)/shard_map/while/body/eval_jaxpr/gqd,kgd->gqk/dot_general | solution.py:142
  247.6 4.8 %fusion.82 = f32[2,1024]{1,0:T(2,128)S(1)} fusion(f32[2,1024,1024]{2,1,0:T(8,128)} %get-tuple-element.407, f32[2,1024]{1,0:T(2,128)S(1)} %fusion.81, pred[1024,1024]{0,1:T(8,128)(4,1)S(1)} %broadcast_compare_fusion.2), kind=kLoop, calls=%fused_computation.11.clone.1 | loop fusion | flops 10483712 | bytes 9453568 | tf_op jit(solution)/shard_map/while/body/eval_jaxpr/reduce_sum | solution.py:149
  252.4 0.1 copy.79
  252.5 1.2 copy-done.1
  253.8 0.2 copy-done.6
  254.0 3.7 %fusion.84 = f32[2,1024,128]{2,1,0:T(8,128)S(1)} fusion(bf16[1024,2,128]{2,0,1:T(8,128)(2,1)S(1)} %bitcast.141, f32[2,1024,1024]{2,1,0:T(8,128)S(1)} %copy-done.1, f32[2,1024]{1,0:T(2,128)S(1)} %fusion.81, pred[1024,1024]{0,1:T(8,128)(4,1)S(1)} %broadcast_compare_fusion.2, f32[2,1024,128]{2,1,0:T(8,128)S(1)} %copy-done.6, ...), kind=kOutput, calls=%fused_computation.15.clone.1 | convolution fusion | flops 548143104 | bytes 12075009 | tf_op jit(solution)/shard_map/while/body/eval_jaxpr/gqk,kgd->gqd/dot_general | solution.py:150
  257.7 1.0 copy-done.7
  258.7 0.6 dynamic_slice.45
  260.0 0.1 fusion.79
  260.0 0.7 broadcast_compare_fusion.2
  260.7 2.8 constant_dynamic-slice_fusion.3
  263.6 5.0 %fusion.80 = (f32[2,1024]{1,0:T(2,128)S(1)}, f32[2,1024,1024]{2,1,0:T(8,128)}) fusion(pred[1024,1024]{0,1:T(8,128)(4,1)S(1)} %broadcast_compare_fusion.2, bf16[1024,2,128]{2,0,1:T(8,128)(2,1)S(1)} %bitcast.142, bf16[2,1024,128]{2,1,0:T(8,128)(2,1)S(1)} %copy-done.8), kind=kOutput, calls=%fused_computation.9.clone.1 | convolution fusion | flops 543160320 | bytes 10493952 | tf_op jit(solution)/shard_map/while/body/eval_jaxpr/gqd,kgd->gqk/dot_general | solution.py:142
  268.6 4.8 %fusion.82 = f32[2,1024]{1,0:T(2,128)S(1)} fusion(f32[2,1024,1024]{2,1,0:T(8,128)} %get-tuple-element.407, f32[2,1024]{1,0:T(2,128)S(1)} %fusion.81, pred[1024,1024]{0,1:T(8,128)(4,1)S(1)} %broadcast_compare_fusion.2), kind=kLoop, calls=%fused_computation.11.clone.1 | loop fusion | flops 10483712 | bytes 9453568 | tf_op jit(solution)/shard_map/while/body/eval_jaxpr/reduce_sum | solution.py:149
  273.6 1.2 copy-done.1
  274.7 0.2 copy-done.6
  274.9 3.7 %fusion.84 = f32[2,1024,128]{2,1,0:T(8,128)S(1)} fusion(bf16[1024,2,128]{2,0,1:T(8,128)(2,1)S(1)} %bitcast.141, f32[2,1024,1024]{2,1,0:T(8,128)S(1)} %copy-done.1, f32[2,1024]{1,0:T(2,128)S(1)} %fusion.81, pred[1024,1024]{0,1:T(8,128)(4,1)S(1)} %broadcast_compare_fusion.2, f32[2,1024,128]{2,1,0:T(8,128)S(1)} %copy-done.6, ...), kind=kOutput, calls=%fused_computation.15.clone.1 | convolution fusion | flops 548143104 | bytes 12075009 | tf_op jit(solution)/shard_map/while/body/eval_jaxpr/gqk,kgd->gqd/dot_general | solution.py:150
  278.7 1.0 copy-done.7
  279.7 1.6 divide_convert_fusion
  281.3 0.4 copy.73
  281.7 1.2 reshape.203
  282.9 18.6 %psum.14 = bf16[2,32]{1,0:T(2,128)(2,1)S(1)} all-reduce(bf16[2,32]{1,0:T(2,128)(2,1)S(1)} %broadcast_select_fusion.1), channel_id=1, replica_groups=mesh['group'=2,'seq'=8,'head'=2] {'seq'}, use_global_device_ids=true, to_apply=%region_3.4 | all-reduce | flops 64 | bytes 256 | tf_op jit(solution)/shard_map/psum | solution.py:40
  301.5 12.5 %all-reduce.2.cloned.1.call-done = bf16[2,32,64,128]{3,2,1,0:T(8,128)(2,1)} async-done(((bf16[2,32,64,128]{3,2,1,0:T(8,128)(2,1)}), bf16[2,32,64,128]{3,2,1,0:T(8,128)(2,1)}) %all-reduce.2.cloned.1.call-update) | async-done | bytes 1048592 | tf_op jit(solution)/shard_map/psum | solution.py:40
  314.0 1.5 slice_add_fusion.1
  315.5 0.6 copy-done.5
  316.1 1.5 fusion.27
  317.6 3.0 copy.58
  320.6 2.4 reshape.214
  (81 shorter events, 0.8 us)
Async XLA Ops:
  7.2 9.5 %copy-start = (bf16[256,128]{1,0:T(8,128)(2,1)S(1)}, bf16[256,128]{1,0:T(8,128)(2,1)}, u32[]{:S(2)}) copy-start(bf16[256,128]{1,0:T(8,128)(2,1)} %param.17) | copy-start | bytes 196612
  7.2 46.0 %all-gather.6.cloned.1.call-start = ((), (), s32[]{:S(2)}) async-start(), calls=%async_computation.1 | async-start | bytes 1179648 | tf_op jit(solution)/shard_map/all_gather | solution.py:124
  7.9 86.4 %all-gather.8.cloned.1.call-start = ((), (), s32[]{:S(2)}) async-start(), calls=%async_computation.2 | async-start | bytes 1179648 | tf_op jit(solution)/shard_map/all_gather | solution.py:125
  8.7 211.5 %all-gather.10.cloned.1.call-start = ((), (), s32[]{:S(2)}) async-start(), calls=%async_computation.3 | async-start | bytes 9437184 | tf_op jit(solution)/shard_map/all_gather | solution.py:18
  14.3 2.2 copy-start.9
  16.5 29.3 %copy-start.3 = (bf16[2,128,32,64]{1,3,2,0:T(8,128)(2,1)}, bf16[2,128,32,64]{1,3,2,0:T(8,128)(2,1)S(1)}, u32[]{:S(2)}) copy-start(bf16[2,128,32,64]{1,3,2,0:T(8,128)(2,1)S(1)} %copy.44) | copy-start | bytes 3145732
  18.8 26.9 %copy-start.10 = (bf16[256,128]{1,0:T(8,128)(2,1)S(1)}, bf16[256,128]{1,0:T(8,128)(2,1)}, u32[]{:S(2)}) copy-start(bf16[256,128]{1,0:T(8,128)(2,1)} %param.18) | copy-start | bytes 196612
  18.8 295.2 %all-reduce.2.cloned.1.call-start = ((), (), s32[]{:S(2)}) async-start(), calls=%async_computation | async-start | bytes 2097152 | tf_op jit(solution)/shard_map/psum | solution.py:40
  239.1 3.5 %copy-start.8 = (bf16[2,1024,128]{2,1,0:T(8,128)(2,1)S(1)}, bf16[2,1024,128]{2,1,0:T(8,128)(2,1)}, u32[]{:S(2)}) copy-start(bf16[2,1024,128]{2,1,0:T(8,128)(2,1)} %get-tuple-element.465) | copy-start | bytes 1572868 | tf_op jit(solution)/shard_map/while
  247.6 4.9 %copy-start.2 = (bf16[1,2,512,2,128]{4,3,2,0,1:T(2,128)(2,1)S(1)}, bf16[1,2,512,2,128]{4,3,2,0,1:T(2,128)(2,1)}, u32[]{:S(2)}) copy-start(bf16[1,2,512,2,128]{4,3,2,0,1:T(2,128)(2,1)} %get-tuple-element.409) | copy-start | bytes 1572868 | tf_op jit(solution)/shard_map/while
  247.6 6.2 %copy-start.1 = (f32[2,1024,1024]{2,1,0:T(8,128)S(1)}, f32[2,1024,1024]{2,1,0:T(8,128)}, u32[]{:S(2)}) copy-start(f32[2,1024,1024]{2,1,0:T(8,128)} %get-tuple-element.407) | copy-start | bytes 25165828 | tf_op jit(solution)/shard_map/while
  247.6 6.4 %copy-start.6 = (f32[2,1024,128]{2,1,0:T(8,128)S(1)}, f32[2,1024,128]{2,1,0:T(8,128)}, u32[]{:S(2)}) copy-start(f32[2,1024,128]{2,1,0:T(8,128)} %get-tuple-element.450) | copy-start | bytes 3145732 | tf_op jit(solution)/shard_map/while
  257.7 1.0 copy-start.7
  260.0 3.5 %copy-start.8 = (bf16[2,1024,128]{2,1,0:T(8,128)(2,1)S(1)}, bf16[2,1024,128]{2,1,0:T(8,128)(2,1)}, u32[]{:S(2)}) copy-start(bf16[2,1024,128]{2,1,0:T(8,128)(2,1)} %get-tuple-element.465) | copy-start | bytes 1572868 | tf_op jit(solution)/shard_map/while
  268.6 4.9 %copy-start.2 = (bf16[1,2,512,2,128]{4,3,2,0,1:T(2,128)(2,1)S(1)}, bf16[1,2,512,2,128]{4,3,2,0,1:T(2,128)(2,1)}, u32[]{:S(2)}) copy-start(bf16[1,2,512,2,128]{4,3,2,0,1:T(2,128)(2,1)} %get-tuple-element.409) | copy-start | bytes 1572868 | tf_op jit(solution)/shard_map/while
  268.6 6.1 %copy-start.1 = (f32[2,1024,1024]{2,1,0:T(8,128)S(1)}, f32[2,1024,1024]{2,1,0:T(8,128)}, u32[]{:S(2)}) copy-start(f32[2,1024,1024]{2,1,0:T(8,128)} %get-tuple-element.407) | copy-start | bytes 25165828 | tf_op jit(solution)/shard_map/while
  268.6 6.3 %copy-start.6 = (f32[2,1024,128]{2,1,0:T(8,128)S(1)}, f32[2,1024,128]{2,1,0:T(8,128)}, u32[]{:S(2)}) copy-start(f32[2,1024,128]{2,1,0:T(8,128)} %get-tuple-element.450) | copy-start | bytes 3145732 | tf_op jit(solution)/shard_map/while
  278.7 1.0 copy-start.7
  314.0 1.5 copy-start.4
  314.0 2.1 copy-start.5
  314.0 2.1 copy-start.11
Sparse Core Ops, SparseCore 0:
  10.2 42.9 all-gather.5
  55.3 38.9 all-gather.7
  96.4 123.6 all-gather.9
  237.8 76.1 all-reduce.1
where the time goes:
time: 330 us
  waiting for transfers between devices  181 us (55%)
  blocking collectives  41.1 us (12%)
  other arithmetic  33.8 us (10%)
  local copies, waits for them, and re-layouts  33.6 us (10%)
  matrix products  24.6 us (7%)
  between operations  14 us (4%)
    all_gather x1, waiting for transfers between devices, carried_in(): lax.all_gather(part.astype(kind), axis)  124 us
    all_gather x1, waiting for transfers between devices, local(): v_piece = lax.all_gather(v_slots, 'seq', axis=1, tiled=True)  39 us
    all_gather x1, blocking collectives, carried_in(): lax.all_gather(part.astype(kind), axis)  22.4 us
    psum x1, blocking collectives, broadcast(): return lax.psum(kept, axis)  18.6 us
    select_n x16, other arithmetic, turn(): return jax.tree.map(lambda a, b: jnp.where(reached, a, b), new, before)  14.3 us
    psum x1, waiting for transfers between devices, broadcast(): return lax.psum(kept, axis)  12.5 us
    dot_general x2, matrix products, per_block(): jnp.einsum('gqd,kgd->gqk', q_flat, k_flat, preferred_element_type=jnp.flo...  10 us
    reduce_sum x2, other arithmetic, per_block(): new_sum = run_sum * rescale + jnp.sum(weights, axis=-1)  9.6 us
  transfers between devices with their start and end apart: 4, of which 4 were waited for; matrix products, arithmetic and copies ran while one was open for 18% of the time, Pallas kernels for 0%

commit v1 on v0

--- a/solution.py
+++ b/solution.py
@@ -69,6 +69,29 @@
 
 
 def local(x_in, step_size, a_log, d_skip, b_in, c_in, queries, key_rows, values):
+
+    def wrap_the_widths(block_here):
+        lane_axis = "seq"
+        built = lax.axis_size(lane_axis)
+        b_now = lax.axis_index(lane_axis)
+        low, outer, passed = (built, b_now, block_here.shape[1])
+        all_values, long_array = (block_here, 1)
+        while long_array < low:
+            all_values = jnp.concatenate(
+                [
+                    all_values,
+                    lax.ppermute(
+                        all_values,
+                        lane_axis,
+                        [(hop_no, (hop_no - long_array) % low) for hop_no in range(low)],
+                    ),
+                ],
+                axis=1,
+            )
+            long_array = 2 * long_array
+        piece_now = jnp.roll(all_values, outer * passed, axis=1)
+        return piece_now
+
     my_index = lax.axis_index("seq")
     seq_count = lax.axis_size("seq")
     tok_rows = x_in.shape[0]
@@ -122,7 +145,7 @@
     )
     running = start_state
     k_piece = lax.all_gather(k_slots, "seq", axis=1, tiled=True)
-    v_piece = lax.all_gather(v_slots, "seq", axis=1, tiled=True)
+    v_piece = wrap_the_widths(v_slots)
     rows = k_piece.shape[1]
     block_rows = 512
     count = rows // block_rows

time: 330 us -> 316 us (0.958)
  waiting for transfers between devices: 181 us -> 142 us
  other arithmetic: 33.8 us -> 47.7 us
  starting transfers between devices: 0.16 us -> 7.68 us
    all_gather x1 -> x0, waiting for transfers between devices: 39 us -> none  [local(): v_piece = lax.all_gather(v_slots, 'seq', axis=1, tiled=True)]
    ppermute x0 -> x3, waiting for transfers between devices: none -> 17.1 us  [wrap_the_widths(): lax.ppermute(all_values, lane_axis, [(hop_no, (hop_no - long_array) % low...]
    all_gather x1, waiting for transfers between devices: 124 us -> 111 us  [carried_in(): lax.all_gather(part.astype(kind), axis)]
    ppermute x0 -> x3, starting transfers between devices: none -> 7.57 us  [wrap_the_widths(): lax.ppermute(all_values, lane_axis, [(hop_no, (hop_no - long_array) % low...]
    convert_element_type x8, other arithmetic: 0.06 us -> 5.26 us  [turn(): part[k].astype(own.dtype)]
    select_n x16, other arithmetic: 14.3 us -> 19.5 us  [turn(): return jax.tree.map(lambda a, b: jnp.where(reached, a, b), new, before)]
    all_gather x1, waiting for transfers between devices: 3.96 us -> 0.01 us  [local(): k_piece = lax.all_gather(k_slots, 'seq', axis=1, tiled=True)]
    unnamed x18 -> x45, local copies, waits for them, and re-layouts: 6.11 us -> 7.52 us
  transfers between devices with their start and end apart: 4 -> 6, of which waited for: 4 -> 4; matrix products, arithmetic and copies ran while one was open for 18% -> 22% of each run, Pallas kernels for 0% -> 0%
where the time goes in v1:
time: 316 us; the launch traced here: 315 us
  waiting for transfers between devices  142 us (45%)
  other arithmetic  47.7 us (15%)
  blocking collectives  39.4 us (12%)
  local copies, waits for them, and re-layouts  36 us (11%)
  matrix products  26.7 us (8%)
  between operations  14 us (4%)
  starting transfers between devices  7.68 us (2%)
    all_gather x1, waiting for transfers between devices, carried_in(): lax.all_gather(part.astype(kind), axis)  111 us
    all_gather x1, blocking collectives, carried_in(): lax.all_gather(part.astype(kind), axis)  20.8 us
    select_n x16, other arithmetic, turn(): return jax.tree.map(lambda a, b: jnp.where(reached, a, b), new, before)  19.5 us
    psum x1, blocking collectives, broadcast(): return lax.psum(kept, axis)  18.6 us
    ppermute x3, waiting for transfers between devices, wrap_the_widths(): lax.ppermute(all_values, lane_axis, [(hop_no, (hop_no - long_array) % low...  17.1 us
    psum x1, waiting for transfers between devices, broadcast(): return lax.psum(kept, axis)  12.4 us
    dot_general x2, matrix products, per_block(): jnp.einsum('gqd,kgd->gqk', q_flat, k_flat, preferred_element_type=jnp.flo...  10.1 us
    reduce_sum x2, other arithmetic, per_block(): new_sum = run_sum * rescale + jnp.sum(weights, axis=-1)  9.6 us
  transfers between devices with their start and end apart: 6, of which 4 were waited for; matrix products, arithmetic and copies ran while one was open for 22% of the time, Pallas kernels for 0%

profile of v1, /device:TPU:0, one launch (start us, length us, event | category | flops | bytes accessed | tf_op | source)
XLA Modules:
  0.0 314.5 jit_solution(10342147192768384529)
XLA Ops:
  7.2 0.7 all-gather.5.cloned.1.call-update
  8.0 0.7 exponential_negate_fusion
  8.6 0.8 broadcast_multiply_fusion
  10.2 3.3 %reshape.215 = bf16[2,128,32,64]{3,2,1,0:T(8,128)(2,1)S(1)} reshape(bf16[256,2048]{1,0:T(8,128)(2,1)} %param.13) | data formatting | bytes 2097152 | tf_op jit(solution)/shard_map/reshape | solution.py:101
  13.6 2.2 copy.44
  15.9 2.2 fusion.48
  18.2 6.0 %collective-permute-start = (bf16[2,128,256]{2,1,0:T(8,128)(2,1)S(1)}, bf16[2,128,256]{2,1,0:T(8,128)(2,1)S(1)}, u32[]{:S(2)}, u32[]{:S(2)}) collective-permute-start(bf16[2,128,256]{2,1,0:T(8,128)(2,1)S(1)} %bitcast.149), channel_id=1, source_target_pairs={{0,14},{2,0},{4,2},{6,4},{8,6},{10,8},{12,10},{14,12},{1,15},{3,1}... | collective-permute-start | bytes 393224 | tf_op jit(solution)/shard_map/ppermute | solution.py:83
  26.7 0.7 constant_dynamic-update-slice_fusion.7
  27.3 1.1 collective-permute-done
  28.5 0.8 pad_maximum_fusion.1
  29.2 1.5 collective-permute-start.1
  31.3 2.2 reshape.198
  33.5 1.9 copy.50
  35.5 0.7 copy.46
  36.1 20.8 %all-gather = bf16[16,32,1]{1,2,0:T(2,128)(2,1)S(1)} all-gather(bf16[2,32,1]{1,2,0:T(2,128)(2,1)S(1)} %copy.46), channel_id=2, replica_groups=mesh['group'=2,'seq'=8,'head'=2] {'seq'}, dimensions={0}, use_global_device_ids=true | all-gather | bytes 1152 | tf_op jit(solution)/shard_map/all_gather | solution.py:18
  57.5 1.0 fusion.49
  58.5 1.0 pad_maximum_fusion
  59.6 4.4 %fusion.24 = f32[2,32,128,64]{2,3,1,0:T(8,128)} fusion(bf16[2,128,32,64]{1,3,2,0:T(8,128)(2,1)S(1)} %copy.44, f32[2,32,128]{2,1,0:T(8,128)} %bitcast_bitcast_fusion.1, f32[2,32,128]{2,1,0:T(8,128)S(1)} %reduce_window_sum.11, f32[2,128,128]{2,1,0:T(8,128)S(1)} %fusion.49, pred[128,128]{1,0:T(8,128)(4,1)} %iota_compare_fusion), kind=kOutput, calls=%fused_computation.35 | convolution fusion | flops 139460608 | bytes 3358720 | tf_op jit(solution)/shard_map/chij,cjhp->cihp/dot_general | solution.py:49
  64.1 15.9 %collective-permute-done.2 = bf16[2,512,256]{2,1,0:T(8,128)(2,1)S(1)} collective-permute-done((bf16[2,512,256]{2,1,0:T(8,128)(2,1)S(1)}, bf16[2,512,256]{2,1,0:T(8,128)(2,1)S(1)}, u32[]{:S(2)}, u32[]{:S(2)}) %collective-permute-start.2) | collective-permute-done | bytes 524320 | tf_op jit(solution)/shard_map/ppermute | solution.py:83
  80.3 1.1 reshape.201
  81.4 2.2 reshape.197
  83.6 111.4 %all-gather.7.cloned.1.call-done = bf16[16,32,64,128]{3,2,1,0:T(8,128)(2,1)} async-done(((bf16[2,32,64,128]{3,2,1,0:T(8,128)(2,1)}), bf16[16,32,64,128]{3,2,1,0:T(8,128)(2,1)}) %all-gather.7.cloned.1.call-update) | async-done | bytes 8388624 | tf_op jit(solution)/shard_map/all_gather | solution.py:18
  195.0 24.8 %while.31 = (s32[]{:T(128)}, f32[2,32]{1,0:T(2,128)S(1)}, f32[2,32,64,128]{3,2,1,0:T(8,128)S(1)}, s32[]{:T(128)}, bf16[8,2,32]{2,1,0:T(2,128)(2,1)}, /*index=5*/...) while((s32[]{:T(128)}, f32[2,32]{1,0:T(2,128)S(1)}, f32[2,32,64,128]{3,2,1,0:T(8,128)S(1)}, ...), condition=%wide.region_2.3_spmd.clone, body=%wide.region_1.2_spmd.clone.sunk | while | flops 2621764 | bytes 5244279 | solution.py:35
  195.0 0.7 bitcast_convert_fusion.2
  195.6 1.8 fusion.73
  197.4 0.7 multiply_select_fusion.2
  198.1 0.7 bitcast_convert_fusion.2
  198.7 1.8 fusion.73
  200.5 0.7 multiply_select_fusion.2
  201.2 0.7 bitcast_convert_fusion.2
  201.8 1.8 fusion.73
  203.6 0.7 multiply_select_fusion.2
  204.9 1.8 fusion.73
  206.7 0.7 multiply_select_fusion.2
  208.0 1.8 fusion.73
  209.8 0.7 multiply_select_fusion.2
  211.1 1.8 fusion.73
  212.9 0.7 multiply_select_fusion.2
  214.2 1.8 fusion.73
  216.0 0.7 multiply_select_fusion.2
  217.3 1.8 fusion.73
  219.1 0.7 multiply_select_fusion.2
  219.8 2.9 fusion.41
  222.7 42.1 %while.32 = (s32[]{:T(128)}, f32[2,1024]{1,0:T(2,128)S(1)}, f32[2,1024]{1,0:T(2,128)S(1)}, f32[2,1024,128]{2,1,0:T(8,128)}, s32[2]{0:T(128)S(1)}, /*index=5*/bf1...) while((s32[]{:T(128)}, f32[2,1024]{1,0:T(2,128)S(1)}, ...), condition=%wide.region_8.9_spmd.clone, body=%wide.region_5.8_spmd.clone.sunk | while | flops 1102851072 | bytes 83518768 | solution.py:179
  224.7 2.7 constant_dynamic-slice_fusion.4
  227.6 5.1 %fusion.80 = (f32[2,1024]{1,0:T(2,128)S(1)}, f32[2,1024,1024]{2,1,0:T(8,128)}) fusion(pred[1024,1024]{0,1:T(8,128)(4,1)S(1)} %broadcast_compare_fusion.2, bf16[1024,2,128]{2,0,1:T(8,128)(2,1)S(1)} %bitcast.142, bf16[2,1024,128]{2,1,0:T(8,128)(2,1)S(1)} %copy-done.13), kind=kOutput, calls=%fused_computation.9.clone.1 | convolution fusion | flops 543160320 | bytes 10493952 | tf_op jit(solution)/shard_map/while/body/eval_jaxpr/gqd,kgd->gqk/dot_general | solution.py:165
  232.7 4.8 %fusion.82 = f32[2,1024]{1,0:T(2,128)S(1)} fusion(f32[2,1024,1024]{2,1,0:T(8,128)} %get-tuple-element.407, f32[2,1024]{1,0:T(2,128)S(1)} %fusion.81, pred[1024,1024]{0,1:T(8,128)(4,1)S(1)} %broadcast_compare_fusion.2), kind=kLoop, calls=%fused_computation.11.clone.1 | loop fusion | flops 10483712 | bytes 9453568 | tf_op jit(solution)/shard_map/while/body/eval_jaxpr/reduce_sum | solution.py:172
  237.6 1.2 copy-done.1
  239.0 3.7 %fusion.84 = f32[2,1024,128]{2,1,0:T(8,128)S(1)} fusion(bf16[1024,2,128]{2,0,1:T(8,128)(2,1)S(1)} %bitcast.141, f32[2,1024,1024]{2,1,0:T(8,128)S(1)} %copy-done.1, f32[2,1024]{1,0:T(2,128)S(1)} %fusion.81, pred[1024,1024]{0,1:T(8,128)(4,1)S(1)} %broadcast_compare_fusion.2, f32[2,1024,128]{2,1,0:T(8,128)S(1)} %copy-done.10, ...), kind=kOutput, calls=%fused_computation.15.clone.1 | convolution fusion | flops 548143104 | bytes 12075009 | tf_op jit(solution)/shard_map/while/body/eval_jaxpr/gqk,kgd->gqd/dot_general | solution.py:173
  242.8 1.0 copy-done.11
  245.8 2.8 constant_dynamic-slice_fusion.4
  248.7 5.1 %fusion.80 = (f32[2,1024]{1,0:T(2,128)S(1)}, f32[2,1024,1024]{2,1,0:T(8,128)}) fusion(pred[1024,1024]{0,1:T(8,128)(4,1)S(1)} %broadcast_compare_fusion.2, bf16[1024,2,128]{2,0,1:T(8,128)(2,1)S(1)} %bitcast.142, bf16[2,1024,128]{2,1,0:T(8,128)(2,1)S(1)} %copy-done.13), kind=kOutput, calls=%fused_computation.9.clone.1 | convolution fusion | flops 543160320 | bytes 10493952 | tf_op jit(solution)/shard_map/while/body/eval_jaxpr/gqd,kgd->gqk/dot_general | solution.py:165
  253.7 4.8 %fusion.82 = f32[2,1024]{1,0:T(2,128)S(1)} fusion(f32[2,1024,1024]{2,1,0:T(8,128)} %get-tuple-element.407, f32[2,1024]{1,0:T(2,128)S(1)} %fusion.81, pred[1024,1024]{0,1:T(8,128)(4,1)S(1)} %broadcast_compare_fusion.2), kind=kLoop, calls=%fused_computation.11.clone.1 | loop fusion | flops 10483712 | bytes 9453568 | tf_op jit(solution)/shard_map/while/body/eval_jaxpr/reduce_sum | solution.py:172
  258.7 1.2 copy-done.1
  260.1 3.7 %fusion.84 = f32[2,1024,128]{2,1,0:T(8,128)S(1)} fusion(bf16[1024,2,128]{2,0,1:T(8,128)(2,1)S(1)} %bitcast.141, f32[2,1024,1024]{2,1,0:T(8,128)S(1)} %copy-done.1, f32[2,1024]{1,0:T(2,128)S(1)} %fusion.81, pred[1024,1024]{0,1:T(8,128)(4,1)S(1)} %broadcast_compare_fusion.2, f32[2,1024,128]{2,1,0:T(8,128)S(1)} %copy-done.10, ...), kind=kOutput, calls=%fused_computation.15.clone.1 | convolution fusion | flops 548143104 | bytes 12075009 | tf_op jit(solution)/shard_map/while/body/eval_jaxpr/gqk,kgd->gqd/dot_general | solution.py:173
  263.8 1.0 copy-done.11
  264.8 1.6 divide_convert_fusion
  266.8 1.2 reshape.203
  268.0 18.6 %psum.14 = bf16[2,32]{1,0:T(2,128)(2,1)S(1)} all-reduce(bf16[2,32]{1,0:T(2,128)(2,1)S(1)} %broadcast_select_fusion.1), channel_id=1, replica_groups=mesh['group'=2,'seq'=8,'head'=2] {'seq'}, use_global_device_ids=true, to_apply=%region_3.4 | all-reduce | flops 64 | bytes 256 | tf_op jit(solution)/shard_map/psum | solution.py:40
  286.7 12.4 %all-reduce.2.cloned.1.call-done = bf16[2,32,64,128]{3,2,1,0:T(8,128)(2,1)} async-done(((bf16[2,32,64,128]{3,2,1,0:T(8,128)(2,1)}), bf16[2,32,64,128]{3,2,1,0:T(8,128)(2,1)}) %all-reduce.2.cloned.1.call-update) | async-done | bytes 1048592 | tf_op jit(solution)/shard_map/psum | solution.py:40
  299.0 1.5 slice_add_fusion.1
  301.1 1.5 fusion.27
  302.6 3.0 copy.58
  305.6 2.4 reshape.214
  (115 shorter events, 12.8 us)
Async XLA Ops:
  7.2 8.7 %copy-start = (bf16[256,128]{1,0:T(8,128)(2,1)S(1)}, bf16[256,128]{1,0:T(8,128)(2,1)}, u32[]{:S(2)}) copy-start(bf16[256,128]{1,0:T(8,128)(2,1)} %param.17) | copy-start | bytes 196612
  7.2 74.2 %all-gather.5.cloned.1.call-start = ((), (), s32[]{:S(2)}) async-start(), calls=%async_computation.1 | async-start | bytes 1179648 | tf_op jit(solution)/shard_map/all_gather | solution.py:147
  7.9 187.1 %all-gather.7.cloned.1.call-start = ((), (), s32[]{:S(2)}) async-start(), calls=%async_computation.2 | async-start | bytes 9437184 | tf_op jit(solution)/shard_map/all_gather | solution.py:18
  10.2 14.6 %copy-start.18 = (f32[2,32,1]{1,0,2:T(2,128)}, f32[2,32,1]{1,0,2:T(2,128)S(1)}, u32[]{:S(2)}) copy-start(f32[2,32,1]{1,0,2:T(2,128)S(1)} %copy.65) | copy-start | bytes 772
  13.5 2.2 copy-start.14
  15.8 43.9 %copy-start.3 = (bf16[2,128,32,64]{1,3,2,0:T(8,128)(2,1)}, bf16[2,128,32,64]{1,3,2,0:T(8,128)(2,1)S(1)}, u32[]{:S(2)}) copy-start(bf16[2,128,32,64]{1,3,2,0:T(8,128)(2,1)S(1)} %copy.44) | copy-start | bytes 3145732
  15.9 2.3 copy-start.6
  18.1 280.9 %all-reduce.2.cloned.1.call-start = ((), (), s32[]{:S(2)}) async-start(), calls=%async_computation | async-start | bytes 2097152 | tf_op jit(solution)/shard_map/psum | solution.py:40
  18.2 10.3 %collective-permute-start = (bf16[2,128,256]{2,1,0:T(8,128)(2,1)S(1)}, bf16[2,128,256]{2,1,0:T(8,128)(2,1)S(1)}, u32[]{:S(2)}, u32[]{:S(2)}) collective-permute-start(bf16[2,128,256]{2,1,0:T(8,128)(2,1)S(1)} %bitcast.149), channel_id=1, source_target_pairs={{0,14},{2,0},{4,2},{6,4},{8,6},{10,8},{12,10},{14,12},{1,15},{3,1}... | collective-permute-start | bytes 393224 | tf_op jit(solution)/shard_map/ppermute | solution.py:83
  28.5 2.9 copy-start.8
  29.2 29.3 %collective-permute-start.1 = (bf16[2,256,256]{2,1,0:T(8,128)(2,1)}, bf16[2,256,256]{2,1,0:T(8,128)(2,1)S(1)}, u32[]{:S(2)}, u32[]{:S(2)}) collective-permute-start(bf16[2,256,256]{2,1,0:T(8,128)(2,1)} %pad_maximum_fusion.1), channel_id=1, source_target_pairs={{0,12},{2,14},{4,0},{6,2},{8,4},{10,6},{12,8},{14,10},{1,13},{3,15... | collective-permute-start | bytes 786440 | tf_op jit(solution)/shard_map/ppermute | solution.py:83
  59.5 4.5 %copy-start.9 = (bf16[2,128,256]{2,1,0:T(8,128)(2,1)S(1)}, bf16[2,128,256]{2,1,0:T(8,128)(2,1)}, u32[]{:S(2)}) copy-start(bf16[2,128,256]{2,1,0:T(8,128)(2,1)} %copy-done.8) | copy-start | bytes 393220
  59.5 4.5 %copy-start.12 = (bf16[2,2048,256]{2,1,0:T(8,128)(2,1)S(1)}, bf16[2,2048,256]{2,1,0:T(8,128)(2,1)}, u32[]{:S(2)}) copy-start(bf16[2,2048,256]{2,1,0:T(8,128)(2,1)} %constant_dynamic-update-slice_fusion.7) | copy-start | bytes 6291460
  59.5 20.5 %copy-start.7 = (bf16[256,256]{1,0:T(8,128)(2,1)S(1)}, bf16[256,256]{1,0:T(8,128)(2,1)}, u32[]{:S(2)}) copy-start(bf16[256,256]{1,0:T(8,128)(2,1)} %param.21) | copy-start | bytes 393220
  59.6 20.5 %collective-permute-start.2 = (bf16[2,512,256]{2,1,0:T(8,128)(2,1)S(1)}, bf16[2,512,256]{2,1,0:T(8,128)(2,1)S(1)}, u32[]{:S(2)}, u32[]{:S(2)}) collective-permute-start(bf16[2,512,256]{2,1,0:T(8,128)(2,1)S(1)} %pad_maximum_fusion), channel_id=1, source_target_pairs={{0,8},{2,10},{4,12},{6,14},{8,0},{10,2},{12,4},{14,6},{1,9},{3,11}... | collective-permute-start | bytes 1572872 | tf_op jit(solution)/shard_map/ppermute | solution.py:83
  80.3 114.7 %copy-start.16 = (f32[2,32]{1,0:T(2,128)S(1)}, f32[2,32]{1,0:T(2,128)}, u32[]{:S(2)}) copy-start(f32[2,32]{1,0:T(2,128)} %custom-call) | copy-start | bytes 772
  195.0 24.8 %copy-start.20 = (f32[2,32]{1,0:T(2,128)S(1)}, f32[2,32]{1,0:T(2,128)}, u32[]{:S(2)}) copy-start(f32[2,32]{1,0:T(2,128)} %bitcast_exponential_fusion) | copy-start | bytes 772
  219.8 3.0 copy-start.17
  224.1 3.5 %copy-start.13 = (bf16[2,1024,128]{2,1,0:T(8,128)(2,1)S(1)}, bf16[2,1024,128]{2,1,0:T(8,128)(2,1)}, u32[]{:S(2)}) copy-start(bf16[2,1024,128]{2,1,0:T(8,128)(2,1)} %get-tuple-element.465) | copy-start | bytes 1572868 | tf_op jit(solution)/shard_map/while
  232.6 4.9 %copy-start.2 = (bf16[1,2,512,2,128]{4,3,2,0,1:T(2,128)(2,1)S(1)}, bf16[1,2,512,2,128]{4,3,2,0,1:T(2,128)(2,1)}, u32[]{:S(2)}) copy-start(bf16[1,2,512,2,128]{4,3,2,0,1:T(2,128)(2,1)} %get-tuple-element.409) | copy-start | bytes 1572868 | tf_op jit(solution)/shard_map/while
  232.6 6.2 %copy-start.1 = (f32[2,1024,1024]{2,1,0:T(8,128)S(1)}, f32[2,1024,1024]{2,1,0:T(8,128)}, u32[]{:S(2)}) copy-start(f32[2,1024,1024]{2,1,0:T(8,128)} %get-tuple-element.407) | copy-start | bytes 25165828 | tf_op jit(solution)/shard_map/while
  232.6 6.4 %copy-start.10 = (f32[2,1024,128]{2,1,0:T(8,128)S(1)}, f32[2,1024,128]{2,1,0:T(8,128)}, u32[]{:S(2)}) copy-start(f32[2,1024,128]{2,1,0:T(8,128)} %get-tuple-element.450) | copy-start | bytes 3145732 | tf_op jit(solution)/shard_map/while
  242.8 1.0 copy-start.11
  245.1 3.5 %copy-start.13 = (bf16[2,1024,128]{2,1,0:T(8,128)(2,1)S(1)}, bf16[2,1024,128]{2,1,0:T(8,128)(2,1)}, u32[]{:S(2)}) copy-start(bf16[2,1024,128]{2,1,0:T(8,128)(2,1)} %get-tuple-element.465) | copy-start | bytes 1572868 | tf_op jit(solution)/shard_map/while
  253.7 4.9 %copy-start.2 = (bf16[1,2,512,2,128]{4,3,2,0,1:T(2,128)(2,1)S(1)}, bf16[1,2,512,2,128]{4,3,2,0,1:T(2,128)(2,1)}, u32[]{:S(2)}) copy-start(bf16[1,2,512,2,128]{4,3,2,0,1:T(2,128)(2,1)} %get-tuple-element.409) | copy-start | bytes 1572868 | tf_op jit(solution)/shard_map/while
  253.7 6.1 %copy-start.1 = (f32[2,1024,1024]{2,1,0:T(8,128)S(1)}, f32[2,1024,1024]{2,1,0:T(8,128)}, u32[]{:S(2)}) copy-start(f32[2,1024,1024]{2,1,0:T(8,128)} %get-tuple-element.407) | copy-start | bytes 25165828 | tf_op jit(solution)/shard_map/while
  253.7 6.3 %copy-start.10 = (f32[2,1024,128]{2,1,0:T(8,128)S(1)}, f32[2,1024,128]{2,1,0:T(8,128)}, u32[]{:S(2)}) copy-start(f32[2,1024,128]{2,1,0:T(8,128)} %get-tuple-element.450) | copy-start | bytes 3145732 | tf_op jit(solution)/shard_map/while
  263.8 1.0 copy-start.11
  264.8 3.2 %copy-start.19 = (f32[2,32,1]{1,0,2:T(2,128)S(1)}, f32[2,32,1]{1,0,2:T(2,128)}, u32[]{:S(2)}) copy-start(f32[2,32,1]{1,0,2:T(2,128)} %copy-done.18) | copy-start | bytes 772
  299.0 1.5 copy-start.4
  299.0 2.1 copy-start.5
  299.0 2.1 copy-start.15
  299.0 2.1 copy-start.21
Sparse Core Ops, SparseCore 0:
  10.2 48.7 all-gather.4
  61.1 133.7 all-gather.6
  222.8 76.1 all-reduce.1
